TPU v7x, 512 devices: a whole 4x8x8 slice. The times are simulated.
512 devices in a mesh: owner: 16 (over x, y_hi), beam: 32 (over y_lo, z, core).
Axes of the slice: x: 4, y: 8 (y_hi: 4, y_lo: 2; y = y_hi * 2 + y_lo), z: 8, core: 2. Of those that a mesh axis runs over, the one named last changes fastest.
Arguments:
- hidden: bfloat16 [4096, 8192], P('owner'), may hold values from -6 to 6
- norm_gain: bfloat16 [8192], replicated, may hold values from 0.099609375 to 1.8984375
- w_qkv: bfloat16 [8192, 10240], P('owner', 'beam'), may hold values from -0.0625 to 0.0625
- w_out: bfloat16 [8192, 8192], P('beam', 'owner'), may hold values from -0.125 to 0.125
- kv_cache: bfloat16 [16384, 2, 8, 1024], P(('owner', 'beam')), may hold values from -384 to 384
- lengths: int32 [4096], P('owner'), may hold values from 1 to 32, 98304 in all
- kept_parent_device: int32 [16384, 1], P('owner'), may hold values from 0 to 31; in each aligned block of 32 rows (0 to 31, 32 to 63, ...) at most 2 rows name the same one
- keep_block: int32 [16384], P('owner'), may hold values from 0 to 31
Outputs:
- mixed: bfloat16 [4096, 8192], P('owner', 'beam')
Inputs may be any that keep to these rules, and one draw needn't show every extreme that they name: `kept_parent_device`: in each aligned block of 32 entries (the new blocks of one device) no value appears more than 2 times, and some value appears exactly 2 times in some block. `lengths`: each entry is at least 1; the largest is exactly 32.
All inputs are finite; a program needn't handle non-finite values. No bound on the sum of `lengths` on one device may be relied on, other than what follows from the above.
Results may differ from a plain program's by a relative error of at most 0.024.
Values may be sent and summed in bfloat16 or wider, within the bound.
No kernel may reach another device: no remote copies, remote signals or barrier semaphores. Data moves between devices by JAX's collectives and lax.ppermute only.
A program may use at most 64 MiB of HBM per device.

v0:
```python
import jax
import jax.numpy as jnp
from jax import lax
from jax.sharding import Mesh
from jax.sharding import PartitionSpec as P

QH = 64
KVH = 8
HD = 128
CACHE = 32
PAGE = 8
QKV = 10240
OWNER = ("x", "yh")
BEAM = ("yl", "z", "c")
PAIR = ("yl", "z")


def rotary_embed(values, positions):
    half = values.shape[-1] // 2
    freqs = 500000.0 ** (-(jnp.arange(half, dtype=jnp.float32) * 2.0) / values.shape[-1])
    angles = positions.astype(jnp.float32)[:, None] * freqs[None, :]
    cosine = jnp.cos(angles)[:, None, :]
    sine = jnp.sin(angles)[:, None, :]
    first = values[..., :half]
    second = values[..., half:]
    return jnp.concatenate(
        [first * cosine - second * sine, second * cosine + first * sine], axis=-1
    )


def regroup(blocks):
    return lax.all_to_all(blocks, BEAM, split_axis=1, concat_axis=1, tiled=True)


def gather_rows(tile, axis, count):
    copies = jnp.broadcast_to(tile[None], (count,) + tile.shape)
    return lax.all_to_all(copies, axis, 0, 0, tiled=True).reshape((-1,) + tile.shape[1:])


def ring_near(piece, axis, count):
    ahead = [(i, (i + 1) % count) for i in range(count)]
    behind = [(i, (i - 1) % count) for i in range(count)]
    return (lax.ppermute(piece, axis, ahead), lax.ppermute(piece, axis, behind))


def ring_far(piece, near, axis, count):
    ahead = [(i, (i + 1) % count) for i in range(count)]
    behind = [(i, (i - 1) % count) for i in range(count)]
    from_left, from_right = near
    cut = piece.shape[0] // 2
    far = jnp.concatenate(
        [lax.ppermute(from_left[:cut], axis, ahead), lax.ppermute(from_right[cut:], axis, behind)],
        axis=0,
    )
    return [piece, from_right, far, from_left]


def attend(queries, fresh_key, value_new, keys, values, positions):
    beams = queries.shape[0]
    grouped_heads = queries.reshape(beams, KVH, QH // KVH, HD)
    scale_factor = HD ** (-0.5)
    scores = (
        jnp.einsum("bkgd,btkd->bkgt", grouped_heads, keys, preferred_element_type=jnp.float32)
        * scale_factor
    )
    local_beam_score = (
        jnp.einsum("rhap,rhp->rha", grouped_heads, fresh_key, preferred_element_type=jnp.float32)
        * scale_factor
    )
    valid = (jnp.arange(keys.shape[1], dtype=jnp.int32)[None, :] < positions[:, None])[
        :, None, None, :
    ]
    scores = jnp.where(valid, scores, -1e30)
    highest = jnp.maximum(jnp.max(scores, axis=-1), local_beam_score)
    weights = jnp.where(valid, jnp.exp(scores - highest[..., None]), 0.0)
    own_weight = jnp.exp(local_beam_score - highest)
    totals = jnp.sum(weights, axis=-1) + own_weight
    probs = (weights / totals[..., None]).astype(jnp.bfloat16)
    own_prob = (own_weight / totals).astype(jnp.bfloat16)
    output = jnp.einsum("bkgt,btkd->bkgd", probs, values, preferred_element_type=jnp.float32)
    output = (
        output
        + own_prob.astype(jnp.float32)[..., None] * value_new.astype(jnp.float32)[:, :, None, :]
    )
    return output.reshape(beams, QH * HD).astype(jnp.bfloat16)


def shards(hidden, norm_gain, w_qkv, w_out, kv_cache, lengths, kept_parent_device, keep_block):
    columns = lax.axis_size(BEAM)
    my_column = lax.axis_index(BEAM)
    grouped_row_block = hidden.shape[0]
    own_beams = grouped_row_block // columns
    cores = lax.axis_size("c")
    core = lax.axis_index("c")
    assert cores == 2
    halves = w_out.reshape(w_out.shape[0], cores, w_out.shape[1] // cores)
    mine = jnp.take(halves, core, axis=1)
    other = lax.ppermute(jnp.take(halves, 1 - core, axis=1), "c", [(0, 1), (1, 0)])
    w_local = jnp.where(
        core == 0, jnp.concatenate([mine, other], 0), jnp.concatenate([other, mine], 0)
    )
    floats = hidden.astype(jnp.float32)
    scale_rms = lax.rsqrt(jnp.mean(floats * floats, axis=-1, keepdims=True) + 1e-05)
    normed = (floats * scale_rms * norm_gain.astype(jnp.float32)).astype(jnp.bfloat16)
    xs = lax.axis_size("x")
    ys = lax.axis_size("yh")
    assert xs == 4 and ys == 4
    me = lax.axis_index("x")
    mine_y = lax.axis_index("yh")
    rows = w_qkv.shape[0]
    wide = 192
    stack = gather_rows(w_qkv[:, :wide], "yh", ys)
    by_x = ring_near(w_qkv[:, wide:], "x", xs)
    near = ring_near(stack, "x", xs)
    w_local, near, by_x = lax.optimization_barrier((w_local, near, by_x))
    w_pair = lax.all_gather(w_local[:, None], OWNER, axis=1, tiled=True)
    stack_b = jnp.concatenate(ring_far(w_qkv[:, wide:], by_x, "x", xs), axis=0)
    pieces_b = ring_far(stack_b, ring_near(stack_b, "yh", ys), "yh", ys)
    pieces_a = ring_far(stack, near, "x", xs)
    part_a = None
    for step, piece in enumerate(pieces_a):
        start = (me + step) % xs * ys * rows
        block = lax.dynamic_slice_in_dim(normed, start, ys * rows, axis=1)
        term = jnp.einsum(
            "jbd,dc->bjc",
            block.reshape(columns, own_beams, ys * rows),
            piece,
            preferred_element_type=jnp.float32,
        )
        part_a = term if part_a is None else part_a + term
    part_b = None
    for step, piece in enumerate(pieces_b):
        block = jnp.concatenate(
            [
                lax.dynamic_slice_in_dim(
                    normed, ((me + dx) % xs * ys + (mine_y + step) % ys) * rows, rows, axis=1
                )
                for dx in range(xs)
            ],
            axis=1,
        )
        term = jnp.einsum(
            "jbd,dc->bjc",
            block.reshape(columns, own_beams, xs * rows),
            piece,
            preferred_element_type=jnp.float32,
        )
        part_b = term if part_b is None else part_b + term
    projected = jnp.concatenate([part_a, part_b], axis=-1)
    own_qkv = regroup(projected.astype(jnp.bfloat16)).reshape(own_beams, QKV)
    blk_dev = kv_cache.shape[0]
    most_slots = max(2, 2 * blk_dev // columns)
    sources = kept_parent_device.reshape(columns, blk_dev)
    picked = keep_block.reshape(columns, blk_dev)
    is_mine = (sources == my_column).astype(jnp.int32)
    ranks = jnp.cumsum(is_mine, axis=1) - 1
    slot_ids = jnp.arange(most_slots, dtype=jnp.int32)
    chosen = is_mine[:, :, None] * (ranks[:, :, None] == slot_ids[None, None, :]).astype(jnp.int32)
    send_table = jnp.sum(chosen * picked[:, :, None], axis=1)
    outgoing = kv_cache[send_table.reshape(-1)].reshape((columns, most_slots) + kv_cache.shape[1:])
    incoming_blocks = lax.all_to_all(outgoing, BEAM, split_axis=0, concat_axis=0, tiled=True)
    own_sources = lax.dynamic_index_in_dim(sources, my_column, 0, keepdims=False)
    one_hot = (own_sources[:, None] == jnp.arange(columns, dtype=jnp.int32)[None, :]).astype(
        jnp.int32
    )
    earlier = jnp.cumsum(one_hot, axis=0) - one_hot
    arrival = jnp.sum(earlier * one_hot, axis=1)
    flat_blocks = incoming_blocks.reshape((columns * most_slots,) + kv_cache.shape[1:])
    moved = flat_blocks[own_sources * most_slots + arrival]
    moved = moved.reshape(own_beams, CACHE // PAGE, 2, PAGE, KVH, HD)
    keys = moved[:, :, 0].reshape(own_beams, CACHE, KVH, HD)
    values = moved[:, :, 1].reshape(own_beams, CACHE, KVH, HD)
    positions = lax.dynamic_slice_in_dim(lengths, my_column * own_beams, own_beams)
    query_cols = own_qkv[:, : QH * HD].reshape(own_beams, QH, HD).astype(jnp.float32)
    key_cols = own_qkv[:, QH * HD : (QH + KVH) * HD].reshape(own_beams, KVH, HD).astype(jnp.float32)
    value_new = own_qkv[:, (QH + KVH) * HD :].reshape(own_beams, KVH, HD)
    queries = rotary_embed(query_cols, positions).astype(jnp.bfloat16)
    fresh_key = rotary_embed(key_cols, positions).astype(jnp.bfloat16)
    attn = attend(queries, fresh_key, value_new, keys, values, positions)
    pairs = columns // cores
    pair_feats = attn.reshape(own_beams, pairs, 1, cores * attn.shape[1] // columns)
    doubled = jnp.broadcast_to(pair_feats, (own_beams, pairs, cores, pair_feats.shape[3]))
    head_rows = lax.all_to_all(
        doubled.reshape(own_beams, columns, pair_feats.shape[3]), BEAM, 1, 1, tiled=True
    )
    block = attn.shape[1] // columns
    partial = None
    for half in range(cores):
        term = (
            jnp.einsum(
                "bjh,hpc->jbpc",
                head_rows[:, :, half * block : (half + 1) * block],
                w_pair[half * block : (half + 1) * block],
                preferred_element_type=jnp.float32,
            )
            .astype(jnp.bfloat16)
            .astype(jnp.float32)
        )
        partial = term if partial is None else partial + term
    partial = partial.astype(jnp.bfloat16).reshape(grouped_row_block, pairs, block)
    spread = lax.all_to_all(partial.transpose(1, 0, 2), PAIR, 0, 0, tiled=True)
    return jnp.sum(spread.astype(jnp.float32), axis=0).astype(jnp.bfloat16)


def solution(mesh):
    sizes = dict(mesh.shape)
    parts = mesh.devices.reshape(4, sizes["owner"] // 4, 2, sizes["beam"] // 4, 2)
    view = Mesh(parts, OWNER + BEAM)
    return jax.shard_map(
        shards,
        mesh=view,
        in_specs=(
            P(OWNER, None),
            P(),
            P(OWNER, BEAM),
            P(BEAM, OWNER),
            P(OWNER + BEAM, None, None, None),
            P(OWNER),
            P(OWNER, None),
            P(OWNER),
        ),
        out_specs=P(OWNER, BEAM),
        check_vma=False,
    )
```

profile of v0, /device:TPU:56, one launch (start us, length us, event | category | flops | bytes accessed | tf_op | source)
XLA Modules:
  0.0 342.8 jit_solution(9053897651199613312)
XLA Ops:
  6.5 1.0 slice.65
  7.7 3.4 collective-permute-start.3
  11.1 3.7 %collective-permute-start.4 = (bf16[512,128]{1,0:T(8,128)(2,1)S(1)}, bf16[512,128]{1,0:T(8,128)(2,1)}, u32[]{:S(2)}, u32[]{:S(2)}) collective-permute-start(bf16[512,128]{1,0:T(8,128)(2,1)S(1)} %copy.153), channel_id=1, source_target_pairs={{0,384},{128,0},{256,128},{384,256},{1,385},{129,1},{257,129},{385... | collective-permute-start | bytes 393224 | tf_op jit(solution)/shard_map/ppermute | solution.py:43
  14.8 1.1 copy.103
  15.9 1.9 collective-permute-start
  17.9 1.0 broadcast_in_dim.29
  18.8 7.0 %all-to-all-start = ((bf16[4,512,192]{1,2,0:T(8,128)(2,1)}), bf16[4,512,192]{1,2,0:T(8,128)(2,1)S(1)}, u32[]{:S(2)}, u32[]{:S(2)}) async-start(bf16[4,512,192]{1,2,0:T(8,128)(2,1)} %broadcast_in_dim.29), calls=%async_computation | async-start | bytes 1572864 | tf_op jit(solution)/shard_map/all_to_all | solution.py:37
  25.8 3.1 fusion
  28.9 0.5 broadcast.203
  29.5 0.7 reduce.4
  30.4 5.3 %fusion.2 = bf16[256,8192]{1,0:T(8,128)(2,1)} fusion(bf16[256,8192]{1,0:T(8,128)(2,1)} %param.10, f32[8192]{0:T(1024)S(1)} %convert_element_type.98, f32[256]{0:T(256)S(1)} %add_rsqrt_fusion), kind=kLoop, calls=%fused_computation.6 | loop fusion | flops 8388608 | bytes 8422400 | tf_op jit(solution)/shard_map/convert_element_type | solution.py:104
  35.8 10.3 %all-to-all-done = bf16[4,512,192]{1,2,0:T(8,128)(2,1)S(1)} async-done(((bf16[4,512,192]{1,2,0:T(8,128)(2,1)}), bf16[4,512,192]{1,2,0:T(8,128)(2,1)S(1)}, u32[]{:S(2)}, u32[]{:S(2)}) %all-to-all-start) | async-done | bytes 786464 | tf_op jit(solution)/shard_map/all_to_all | solution.py:37
  46.2 1.9 collective-permute-start.1
  48.1 5.1 %collective-permute-start.2 = (bf16[2048,192]{0,1:T(8,128)(2,1)S(1)}, bf16[2048,192]{0,1:T(8,128)(2,1)}, u32[]{:S(2)}, u32[]{:S(2)}) collective-permute-start(bf16[2048,192]{0,1:T(8,128)(2,1)S(1)} %bitcast.157), channel_id=1, source_target_pairs={{0,384},{128,0},{256,128},{384,256},{1,385},{129,1},{257,129},{385... | collective-permute-start | bytes 2359304 | tf_op jit(solution)/shard_map/ppermute | solution.py:43
  53.2 4.4 %constant_dynamic-slice_fusion.16 = (bf16[256,512]{1,0:T(8,128)(2,1)}, bf16[256,512]{1,0:T(8,128)(2,1)}, bf16[256,512]{1,0:T(8,128)(2,1)}, bf16[256,512]{1,0:T(8...) fusion(bf16[256,8192]{1,0:T(8,128)(2,1)} %fusion.2, ...), kind=kLoop, calls=%fused_computation.145 | loop fusion | bytes 8388672 | tf_op jit(solution)/shard_map/dynamic_slice | solution.py:135
  57.7 1.8 dynamic-slice_bitcast_fusion.2
  59.5 0.7 constant_dynamic-update-slice_fusion.4
  60.4 0.7 reshape.253
  61.1 0.8 maximum_select_fusion
  61.9 0.6 copy.106
  62.5 0.6 reshape.338
  63.1 1.1 slice.67
  64.2 3.1 collective-permute-start.5
  67.3 1.8 slice.68
  69.1 4.0 %collective-permute-start.6 = (bf16[1024,192]{0,1:T(8,128)(2,1)}, bf16[1024,192]{0,1:T(8,128)(2,1)}, u32[]{:S(2)}, u32[]{:S(2)}) collective-permute-start(bf16[1024,192]{0,1:T(8,128)(2,1)} %slice.68), channel_id=1, source_target_pairs={{0,384},{128,0},{256,128},{384,256},{1,385},{129,1},{257,129},{385... | collective-permute-start | bytes 1179656 | tf_op jit(solution)/shard_map/ppermute | solution.py:52
  73.1 2.3 fusion.42
  75.5 2.8 fusion.46
  78.3 1.5 slice.69
  79.8 1.9 collective-permute-start.7
  81.7 1.6 constant_dynamic-update-slice_fusion.3
  83.3 1.5 slice.70
  84.7 5.1 %collective-permute-start.8 = (bf16[256,128]{1,0:T(8,128)(2,1)}, bf16[256,128]{1,0:T(8,128)(2,1)}, u32[]{:S(2)}, u32[]{:S(2)}) collective-permute-start(bf16[256,128]{1,0:T(8,128)(2,1)} %slice.70), channel_id=1, source_target_pairs={{0,384},{128,0},{256,128},{384,256},{1,385},{129,1},{257,129},{385... | collective-permute-start | bytes 196616 | tf_op jit(solution)/shard_map/ppermute | solution.py:52
  89.9 1.5 constant_dynamic-update-slice_fusion.2
  91.4 0.7 collective-permute-done.8
  92.1 1.5 constant_dynamic-update-slice_fusion.1
  93.5 1.6 constant_dynamic-update-slice_fusion
  95.1 4.2 %collective-permute-start.9 = (bf16[2048,128]{1,0:T(8,128)(2,1)}, bf16[2048,128]{1,0:T(8,128)(2,1)S(1)}, u32[]{:S(2)}, u32[]{:S(2)}) collective-permute-start(bf16[2048,128]{1,0:T(8,128)(2,1)} %constant_dynamic-update-slice_fusion), channel_id=1, source_target_pairs={{0,96},{32,0},{64,32},{96,64},{1,97},{33,1},{65,33},{97,65},{2,98}... | collective-permute-start | bytes 1572872 | tf_op jit(solution)/shard_map/ppermute | solution.py:43
  99.3 4.5 %collective-permute-start.10 = (bf16[2048,128]{1,0:T(8,128)(2,1)}, bf16[2048,128]{1,0:T(8,128)(2,1)S(1)}, u32[]{:S(2)}, u32[]{:S(2)}) collective-permute-start(bf16[2048,128]{1,0:T(8,128)(2,1)} %constant_dynamic-update-slice_fusion), channel_id=1, source_target_pairs={{0,32},{32,64},{64,96},{96,0},{1,33},{33,65},{65,97},{97,1},{2,34}... | collective-permute-start | bytes 1572872 | tf_op jit(solution)/shard_map/ppermute | solution.py:43
  103.8 2.0 fusion.44
  105.9 2.1 fusion.8
  108.0 14.6 %collective-permute-done.10 = bf16[2048,128]{1,0:T(8,128)(2,1)S(1)} collective-permute-done((bf16[2048,128]{1,0:T(8,128)(2,1)}, bf16[2048,128]{1,0:T(8,128)(2,1)S(1)}, u32[]{:S(2)}, u32[]{:S(2)}) %collective-permute-start.10) | collective-permute-done | bytes 524320 | tf_op jit(solution)/shard_map/ppermute | solution.py:43
  122.6 1.9 collective-permute-start.11
  124.6 4.8 %collective-permute-start.12 = (bf16[1024,128]{1,0:T(8,128)(2,1)S(1)}, bf16[1024,128]{1,0:T(8,128)(2,1)S(1)}, u32[]{:S(2)}, u32[]{:S(2)}) collective-permute-start(bf16[1024,128]{1,0:T(8,128)(2,1)S(1)} %slice.102), channel_id=1, source_target_pairs={{0,96},{32,0},{64,32},{96,64},{1,97},{33,1},{65,33},{97,65},{2,98}... | collective-permute-start | bytes 786440 | tf_op jit(solution)/shard_map/ppermute | solution.py:52
  129.9 0.5 copy-done.12
  131.1 8.0 %collective-permute-done.11 = bf16[1024,128]{1,0:T(8,128)(2,1)S(1)} collective-permute-done((bf16[1024,128]{1,0:T(8,128)(2,1)S(1)}, bf16[1024,128]{1,0:T(8,128)(2,1)S(1)}, u32[]{:S(2)}, u32[]{:S(2)}) %collective-permute-start.11) | collective-permute-done | bytes 262176 | tf_op jit(solution)/shard_map/ppermute | solution.py:52
  139.6 0.5 copy-done.4
  140.3 1.5 fusion.13
  141.8 0.8 pad_maximum_fusion
  142.6 40.6 %all-to-all-start.1 = ((bf16[8,32,320]{2,0,1:T(8,128)(2,1)}), bf16[8,32,320]{2,0,1:T(8,128)(2,1)S(1)}, u32[]{:S(2)}, u32[]{:S(2)}) async-start(bf16[8,32,320]{2,0,1:T(8,128)(2,1)} %pad_maximum_fusion), calls=%async_computation.1 | async-start | bytes 393216 | tf_op jit(solution)/shard_map/all_to_all | solution.py:32
  183.3 2.0 gather_fusion
  185.4 12.0 %all-to-all-done.1 = bf16[8,32,320]{2,0,1:T(8,128)(2,1)S(1)} async-done(((bf16[8,32,320]{2,0,1:T(8,128)(2,1)}), bf16[8,32,320]{2,0,1:T(8,128)(2,1)S(1)}, u32[]{:S(2)}, u32[]{:S(2)}) %all-to-all-start.1) | async-done | bytes 163872 | tf_op jit(solution)/shard_map/all_to_all | solution.py:32
  197.4 3.9 %all-to-all-start.2 = ((bf16[32,2,2,8,1024]{4,3,2,1,0:T(8,128)(2,1)}), bf16[32,2,2,8,1024]{4,3,2,1,0:T(8,128)(2,1)S(1)}, u32[]{:S(2)}, u32[]{:S(2)}) async-start(bf16[32,2,2,8,1024]{4,3,2,1,0:T(8,128)(2,1)} %bitcast.30), calls=%async_computation.2 | async-start | bytes 4194304 | tf_op jit(solution)/shard_map/all_to_all | solution.py:161
  202.9 48.5 %all-to-all-done.2 = bf16[32,2,2,8,1024]{4,3,2,1,0:T(8,128)(2,1)S(1)} async-done(((bf16[32,2,2,8,1024]{4,3,2,1,0:T(8,128)(2,1)}), bf16[32,2,2,8,1024]{4,3,2,1,0:T(8,128)(2,1)S(1)}, u32[]{:S(2)}, u32[]{:S(2)}) %all-to-all-start.2) | async-done | bytes 2097184 | tf_op jit(solution)/shard_map/all_to_all | solution.py:161
  251.4 1.6 gather_fusion.1
  253.0 1.5 copy.159
  254.6 0.5 fusion.95
  256.0 19.9 %all_to_all.25 = bf16[8,32,512]{2,0,1:T(8,128)(2,1)S(1)} all-to-all(bf16[8,32,512]{2,0,1:T(8,128)(2,1)S(1)} %bitcast.155), channel_id=1, replica_groups=mesh['x'=4,'yh'=4,'yl'=2,'z'=8,'c'=2] {'yl','z','c'}, dimensions={1} | all-to-all | bytes 524288 | tf_op jit(solution)/shard_map/all_to_all | solution.py:183
  275.9 2.5 fusion.91
  278.4 0.7 fusion.66
  279.1 0.7 fusion.3
  279.9 1.2 copy.134
  281.1 0.7 copy.135
  281.8 53.2 %all_to_all.26 = bf16[16,256,256]{2,1,0:T(8,128)(2,1)S(1)} all-to-all(bf16[16,256,256]{2,1,0:T(8,128)(2,1)S(1)} %copy.135), channel_id=1, replica_groups=mesh['x'=4,'yh'=4,'yl'=2,'z'=8,'c'=2] {'yl','z'}, dimensions={0} | all-to-all | bytes 4194304 | tf_op jit(solution)/shard_map/all_to_all | solution.py:201
  335.0 1.0 reduce_sum.55
  (113 shorter events, 5.3 us)
Async XLA Ops:
  6.5 176.8 %copy-start = (bf16[32,2,8,1024]{3,2,1,0:T(8,128)(2,1)S(1)}, bf16[32,2,8,1024]{3,2,1,0:T(8,128)(2,1)}, u32[]{:S(2)}) copy-start(bf16[32,2,8,1024]{3,2,1,0:T(8,128)(2,1)} %param.14) | copy-start | bytes 3145732
  6.5 11.3 %slice-start = ((bf16[512,320]{0,1:T(8,128)(2,1)}), bf16[512,192]{0,1:T(8,128)(2,1)S(1)}, s32[]{:S(2)}) async-start(bf16[512,320]{0,1:T(8,128)(2,1)} %param.12), calls=%async_computation.6 | async-start | bytes 393216 | tf_op jit(solution)/shard_map/slice | solution.py:112
  7.7 55.4 %collective-permute-start.3 = (bf16[512,128]{1,0:T(8,128)(2,1)S(1)}, bf16[512,128]{1,0:T(8,128)(2,1)}, u32[]{:S(2)}, u32[]{:S(2)}) collective-permute-start(bf16[512,128]{1,0:T(8,128)(2,1)S(1)} %copy.153), channel_id=1, source_target_pairs={{0,128},{128,256},{256,384},{384,0},{1,129},{129,257},{257,385},{3... | collective-permute-start | bytes 393224 | tf_op jit(solution)/shard_map/ppermute | solution.py:43
  11.1 52.0 %collective-permute-start.4 = (bf16[512,128]{1,0:T(8,128)(2,1)S(1)}, bf16[512,128]{1,0:T(8,128)(2,1)}, u32[]{:S(2)}, u32[]{:S(2)}) collective-permute-start(bf16[512,128]{1,0:T(8,128)(2,1)S(1)} %copy.153), channel_id=1, source_target_pairs={{0,384},{128,0},{256,128},{384,256},{1,385},{129,1},{257,129},{385... | collective-permute-start | bytes 393224 | tf_op jit(solution)/shard_map/ppermute | solution.py:43
  14.8 11.0 %copy-start.21 = (bf16[8192]{0:T(1024)(128)(2,1)S(1)}, bf16[8192]{0:T(1024)(128)(2,1)}, u32[]{:S(2)}) copy-start(bf16[8192]{0:T(1024)(128)(2,1)} %param.11) | copy-start | bytes 49156
  15.9 45.2 %collective-permute-start = (bf16[256,256]{0,1:T(8,128)(2,1)S(1)}, bf16[256,256]{0,1:T(8,128)(2,1)S(1)}, u32[]{:S(2)}, u32[]{:S(2)}) collective-permute-start(bf16[256,256]{0,1:T(8,128)(2,1)S(1)} %get-tuple-element.59), channel_id=1, source_target_pairs={{0,1},{1,0},{2,3},{3,2},{4,5},{5,4},{6,7},{7,6},{8,9},{9,8},{10,11... | collective-permute-start | bytes 393224 | tf_op jit(solution)/shard_map/ppermute | solution.py:98
  18.8 27.3 %all-to-all-start = ((bf16[4,512,192]{1,2,0:T(8,128)(2,1)}), bf16[4,512,192]{1,2,0:T(8,128)(2,1)S(1)}, u32[]{:S(2)}, u32[]{:S(2)}) async-start(bf16[4,512,192]{1,2,0:T(8,128)(2,1)} %broadcast_in_dim.29), calls=%async_computation | async-start | bytes 1572864 | tf_op jit(solution)/shard_map/all_to_all | solution.py:37
  25.8 250.1 %all-gather.3.cloned.1.call-start = ((), (), s32[]{:S(2)}) async-start(), calls=%async_computation.5 | async-start | bytes 4456448 | tf_op jit(solution)/shard_map/all_gather | solution.py:116
  25.8 3.7 %copy-start.23 = (s32[1024,1]{0,1:T(1,128)S(1)}, s32[1024,1]{0,1:T(1,128)}, u32[]{:S(2)}) copy-start(s32[1024,1]{0,1:T(1,128)} %param.16) | copy-start | bytes 12292
  46.2 17.0 %collective-permute-start.1 = (bf16[2048,192]{0,1:T(8,128)(2,1)S(1)}, bf16[2048,192]{0,1:T(8,128)(2,1)}, u32[]{:S(2)}, u32[]{:S(2)}) collective-permute-start(bf16[2048,192]{0,1:T(8,128)(2,1)S(1)} %bitcast.156), channel_id=1, source_target_pairs={{0,128},{128,256},{256,384},{384,0},{1,129},{129,257},{257,385},{3... | collective-permute-start | bytes 2359304 | tf_op jit(solution)/shard_map/ppermute | solution.py:43
  48.1 15.0 %collective-permute-start.2 = (bf16[2048,192]{0,1:T(8,128)(2,1)S(1)}, bf16[2048,192]{0,1:T(8,128)(2,1)}, u32[]{:S(2)}, u32[]{:S(2)}) collective-permute-start(bf16[2048,192]{0,1:T(8,128)(2,1)S(1)} %bitcast.157), channel_id=1, source_target_pairs={{0,384},{128,0},{256,128},{384,256},{1,385},{129,1},{257,129},{385... | collective-permute-start | bytes 2359304 | tf_op jit(solution)/shard_map/ppermute | solution.py:43
  53.2 4.4 %copy-start.1 = (bf16[256,8192]{1,0:T(8,128)(2,1)S(1)}, bf16[256,8192]{1,0:T(8,128)(2,1)}, u32[]{:S(2)}) copy-start(bf16[256,8192]{1,0:T(8,128)(2,1)} %fusion.2) | copy-start | bytes 12582916
  57.7 2.5 copy-start.22
  63.1 12.4 %copy-start.3 = (bf16[32,8,2048]{2,1,0:T(8,128)(2,1)S(1)}, bf16[32,8,2048]{2,1,0:T(8,128)(2,1)}, u32[]{:S(2)}) copy-start(bf16[32,8,2048]{2,1,0:T(8,128)(2,1)} %get-tuple-element.31) | copy-start | bytes 3145732
  64.2 39.5 %collective-permute-start.5 = (bf16[1024,192]{0,1:T(8,128)(2,1)S(1)}, bf16[1024,192]{0,1:T(8,128)(2,1)}, u32[]{:S(2)}, u32[]{:S(2)}) collective-permute-start(bf16[1024,192]{0,1:T(8,128)(2,1)S(1)} %slice.67), channel_id=1, source_target_pairs={{0,128},{128,256},{256,384},{384,0},{1,129},{129,257},{257,385},{3... | collective-permute-start | bytes 1179656 | tf_op jit(solution)/shard_map/ppermute | solution.py:52
  69.1 34.7 %collective-permute-start.6 = (bf16[1024,192]{0,1:T(8,128)(2,1)}, bf16[1024,192]{0,1:T(8,128)(2,1)}, u32[]{:S(2)}, u32[]{:S(2)}) collective-permute-start(bf16[1024,192]{0,1:T(8,128)(2,1)} %slice.68), channel_id=1, source_target_pairs={{0,384},{128,0},{256,128},{384,256},{1,385},{129,1},{257,129},{385... | collective-permute-start | bytes 1179656 | tf_op jit(solution)/shard_map/ppermute | solution.py:52
  75.5 28.3 %copy-start.2 = (bf16[32,8,2048]{2,1,0:T(8,128)(2,1)S(1)}, bf16[32,8,2048]{2,1,0:T(8,128)(2,1)}, u32[]{:S(2)}) copy-start(bf16[32,8,2048]{2,1,0:T(8,128)(2,1)} %get-tuple-element.33) | copy-start | bytes 3145732
  79.8 10.1 %collective-permute-start.7 = (bf16[256,128]{1,0:T(8,128)(2,1)}, bf16[256,128]{1,0:T(8,128)(2,1)}, u32[]{:S(2)}, u32[]{:S(2)}) collective-permute-start(bf16[256,128]{1,0:T(8,128)(2,1)} %slice.69), channel_id=1, source_target_pairs={{0,128},{128,256},{256,384},{384,0},{1,129},{129,257},{257,385},{3... | collective-permute-start | bytes 196616 | tf_op jit(solution)/shard_map/ppermute | solution.py:52
  84.7 7.3 %collective-permute-start.8 = (bf16[256,128]{1,0:T(8,128)(2,1)}, bf16[256,128]{1,0:T(8,128)(2,1)}, u32[]{:S(2)}, u32[]{:S(2)}) collective-permute-start(bf16[256,128]{1,0:T(8,128)(2,1)} %slice.70), channel_id=1, source_target_pairs={{0,384},{128,0},{256,128},{384,256},{1,385},{129,1},{257,129},{385... | collective-permute-start | bytes 196616 | tf_op jit(solution)/shard_map/ppermute | solution.py:52
  95.1 29.5 %collective-permute-start.9 = (bf16[2048,128]{1,0:T(8,128)(2,1)}, bf16[2048,128]{1,0:T(8,128)(2,1)S(1)}, u32[]{:S(2)}, u32[]{:S(2)}) collective-permute-start(bf16[2048,128]{1,0:T(8,128)(2,1)} %constant_dynamic-update-slice_fusion), channel_id=1, source_target_pairs={{0,96},{32,0},{64,32},{96,64},{1,97},{33,1},{65,33},{97,65},{2,98}... | collective-permute-start | bytes 1572872 | tf_op jit(solution)/shard_map/ppermute | solution.py:43
  99.3 23.3 %collective-permute-start.10 = (bf16[2048,128]{1,0:T(8,128)(2,1)}, bf16[2048,128]{1,0:T(8,128)(2,1)S(1)}, u32[]{:S(2)}, u32[]{:S(2)}) collective-permute-start(bf16[2048,128]{1,0:T(8,128)(2,1)} %constant_dynamic-update-slice_fusion), channel_id=1, source_target_pairs={{0,32},{32,64},{64,96},{96,0},{1,33},{33,65},{65,97},{97,1},{2,34}... | collective-permute-start | bytes 1572872 | tf_op jit(solution)/shard_map/ppermute | solution.py:43
  103.8 2.0 copy-start.20
  105.9 23.6 %copy-start.16 = (bf16[256,512]{1,0:T(8,128)(2,1)S(1)}, bf16[256,512]{1,0:T(8,128)(2,1)}, u32[]{:S(2)}) copy-start(bf16[256,512]{1,0:T(8,128)(2,1)} %get-tuple-element.43) | copy-start | bytes 786436
  105.9 23.6 %copy-start.17 = (bf16[256,512]{1,0:T(8,128)(2,1)S(1)}, bf16[256,512]{1,0:T(8,128)(2,1)}, u32[]{:S(2)}) copy-start(bf16[256,512]{1,0:T(8,128)(2,1)} %get-tuple-element.44) | copy-start | bytes 786436
  105.9 23.6 %copy-start.18 = (bf16[256,512]{1,0:T(8,128)(2,1)S(1)}, bf16[256,512]{1,0:T(8,128)(2,1)}, u32[]{:S(2)}) copy-start(bf16[256,512]{1,0:T(8,128)(2,1)} %get-tuple-element.45) | copy-start | bytes 786436
  105.9 23.6 %copy-start.19 = (bf16[256,512]{1,0:T(8,128)(2,1)S(1)}, bf16[256,512]{1,0:T(8,128)(2,1)}, u32[]{:S(2)}) copy-start(bf16[256,512]{1,0:T(8,128)(2,1)} %get-tuple-element.46) | copy-start | bytes 786436
  122.6 16.5 %collective-permute-start.11 = (bf16[1024,128]{1,0:T(8,128)(2,1)S(1)}, bf16[1024,128]{1,0:T(8,128)(2,1)S(1)}, u32[]{:S(2)}, u32[]{:S(2)}) collective-permute-start(bf16[1024,128]{1,0:T(8,128)(2,1)S(1)} %slice.101), channel_id=1, source_target_pairs={{0,32},{32,64},{64,96},{96,0},{1,33},{33,65},{65,97},{97,1},{2,34}... | collective-permute-start | bytes 786440 | tf_op jit(solution)/shard_map/ppermute | solution.py:52
  124.6 14.5 %collective-permute-start.12 = (bf16[1024,128]{1,0:T(8,128)(2,1)S(1)}, bf16[1024,128]{1,0:T(8,128)(2,1)S(1)}, u32[]{:S(2)}, u32[]{:S(2)}) collective-permute-start(bf16[1024,128]{1,0:T(8,128)(2,1)S(1)} %slice.102), channel_id=1, source_target_pairs={{0,96},{32,0},{64,32},{96,64},{1,97},{33,1},{65,33},{97,65},{2,98}... | collective-permute-start | bytes 786440 | tf_op jit(solution)/shard_map/ppermute | solution.py:52
  129.5 1.0 copy-start.12
  129.5 1.0 copy-start.13
  129.5 1.1 copy-start.14
  129.5 1.2 copy-start.15
  130.6 8.5 %copy-start.8 = (bf16[256,512]{1,0:T(8,128)(2,1)S(1)}, bf16[256,512]{1,0:T(8,128)(2,1)}, u32[]{:S(2)}) copy-start(bf16[256,512]{1,0:T(8,128)(2,1)} %get-tuple-element.39) | copy-start | bytes 786436
  130.7 8.5 %copy-start.9 = (bf16[256,512]{1,0:T(8,128)(2,1)S(1)}, bf16[256,512]{1,0:T(8,128)(2,1)}, u32[]{:S(2)}) copy-start(bf16[256,512]{1,0:T(8,128)(2,1)} %get-tuple-element.40) | copy-start | bytes 786436
  130.7 8.5 %copy-start.10 = (bf16[256,512]{1,0:T(8,128)(2,1)S(1)}, bf16[256,512]{1,0:T(8,128)(2,1)}, u32[]{:S(2)}) copy-start(bf16[256,512]{1,0:T(8,128)(2,1)} %get-tuple-element.41) | copy-start | bytes 786436
  130.7 8.5 %copy-start.11 = (bf16[256,512]{1,0:T(8,128)(2,1)S(1)}, bf16[256,512]{1,0:T(8,128)(2,1)}, u32[]{:S(2)}) copy-start(bf16[256,512]{1,0:T(8,128)(2,1)} %get-tuple-element.42) | copy-start | bytes 786436
  139.1 1.0 copy-start.4
  139.2 1.0 copy-start.5
  139.2 1.1 copy-start.6
  139.2 1.2 copy-start.7
  140.3 42.9 %copy-start.24 = (s32[64,1]{0,1:T(1,128)S(1)}, s32[64,1]{0,1:T(1,128)}, u32[]{:S(2)}) copy-start(s32[64,1]{0,1:T(1,128)} %reshape.253) | copy-start | bytes 772
  142.6 54.7 %all-to-all-start.1 = ((bf16[8,32,320]{2,0,1:T(8,128)(2,1)}), bf16[8,32,320]{2,0,1:T(8,128)(2,1)S(1)}, u32[]{:S(2)}, u32[]{:S(2)}) async-start(bf16[8,32,320]{2,0,1:T(8,128)(2,1)} %pad_maximum_fusion), calls=%async_computation.1 | async-start | bytes 393216 | tf_op jit(solution)/shard_map/all_to_all | solution.py:32
  197.4 4.1 %copy-start.25 = (s32[256]{0:T(256)S(1)}, s32[256]{0:T(256)}, u32[]{:S(2)}) copy-start(s32[256]{0:T(256)} %param.15) | copy-start | bytes 3076
  197.4 54.0 %all-to-all-start.2 = ((bf16[32,2,2,8,1024]{4,3,2,1,0:T(8,128)(2,1)}), bf16[32,2,2,8,1024]{4,3,2,1,0:T(8,128)(2,1)S(1)}, u32[]{:S(2)}, u32[]{:S(2)}) async-start(bf16[32,2,2,8,1024]{4,3,2,1,0:T(8,128)(2,1)} %bitcast.30), calls=%async_computation.2 | async-start | bytes 4194304 | tf_op jit(solution)/shard_map/all_to_all | solution.py:161
Sparse Core Ops, SparseCore 0:
  90.0 103.1 all-gather.2
where the time goes:
time: 344 us; the launch traced here: 343 us
  starting transfers between devices  97.2 us (28%)
  waiting for transfers between devices  94.1 us (27%)
  blocking collectives  73.1 us (21%)
  local copies, waits for them, and re-layouts  36.3 us (11%)
  matrix products  14.7 us (4%)
  between operations  14.3 us (4%)
  other arithmetic  13.2 us (4%)
    all_to_all x1, blocking collectives, shards(): spread = lax.all_to_all(partial.transpose(1, 0, 2), PAIR, 0, 0, tiled=True)  53.2 us
    all_to_all x1, waiting for transfers between devices, shards(): lax.all_to_all(outgoing, BEAM, split_axis=0, concat_axis=0, tiled=True)  48.5 us
    all_to_all x1, starting transfers between devices, regroup(): return lax.all_to_all(blocks, BEAM, split_axis=1, concat_axis=1, tiled=True)  40.6 us
    ppermute x6, starting transfers between devices, ring_near(): return (lax.ppermute(piece, axis, ahead), lax.ppermute(piece, axis, behind))  22.8 us
    all_to_all x1, blocking collectives, shards(): lax.all_to_all(doubled.reshape(own_beams, columns, pair_feats.shape[3]),...  19.9 us
    ppermute x6, waiting for transfers between devices, ring_near(): return (lax.ppermute(piece, axis, ahead), lax.ppermute(piece, axis, behind))  14.6 us
    ppermute x3, starting transfers between devices, ring_far(): lax.ppermute(from_right[cut:], axis, behind)  14 us
    all_to_all x1, waiting for transfers between devices, regroup(): return lax.all_to_all(blocks, BEAM, split_axis=1, concat_axis=1, tiled=True)  12 us
  transfers between devices with their start and end apart: 17, of which 6 were waited for; matrix products, arithmetic and copies ran while one was open for 16% of the time, Pallas kernels for 0%

commit v1 on v0

--- a/solution.py
+++ b/solution.py
@@ -180,9 +180,10 @@
     pairs = columns // cores
     pair_feats = attn.reshape(own_beams, pairs, 1, cores * attn.shape[1] // columns)
     doubled = jnp.broadcast_to(pair_feats, (own_beams, pairs, cores, pair_feats.shape[3]))
-    head_rows = lax.all_to_all(
-        doubled.reshape(own_beams, columns, pair_feats.shape[3]), BEAM, 1, 1, tiled=True
-    )
+    block_2 = doubled.reshape(own_beams, columns, pair_feats.shape[3])
+    cells = jnp.split(block_2, lax.axis_size(BEAM), axis=1)
+    arrived = lax.all_to_all(jnp.stack(cells), BEAM, 0, 0)
+    head_rows = jnp.concatenate(arrived, axis=1)
     block = attn.shape[1] // columns
     partial = None
     for half in range(cores):

time: 344 us -> 331 us (0.962)
  blocking collectives: 73.1 us -> 89.9 us
  starting transfers between devices: 97.2 us -> 80.6 us
  local copies, waits for them, and re-layouts: 36.3 us -> 30.4 us
  waiting for transfers between devices: 94.1 us -> 88.3 us
    all_to_all x1, starting transfers between devices: 40.6 us -> 22.4 us  [regroup(): return lax.all_to_all(blocks, BEAM, split_axis=1, concat_axis=1, tiled=True)]
    all_to_all x1, blocking collectives: 19.9 us -> 29.8 us  [shards(): arrived = lax.all_to_all(jnp.stack(cells), BEAM, 0, 0)]
    all_to_all x1, blocking collectives: 53.2 us -> 60 us  [shards(): spread = lax.all_to_all(partial.transpose(1, 0, 2), PAIR, 0, 0, tiled=True)]
    ppermute x3, waiting for transfers between devices: 8.01 us -> 2.75 us  [ring_far(): lax.ppermute(from_left[:cut], axis, ahead)]
    all_to_all x1, waiting for transfers between devices: 12 us -> 7.87 us  [regroup(): return lax.all_to_all(blocks, BEAM, split_axis=1, concat_axis=1, tiled=True)]
    all_gather x1, waiting for transfers between devices: 0.02 us -> 3.74 us  [shards(): w_pair = lax.all_gather(w_local[:, None], OWNER, axis=1, tiled=True)]
    unnamed x60 -> x91, local copies, waits for them, and re-layouts: 9.86 us -> 6.5 us
  transfers between devices with their start and end apart: 17 -> 17, of which waited for: 6 -> 8; matrix products, arithmetic and copies ran while one was open for 16% -> 13% of each run, Pallas kernels for 0% -> 0%
where the time goes in v1:
time: 331 us; the launch traced here: 329 us
  blocking collectives  89.9 us (27%)
  waiting for transfers between devices  88.3 us (27%)
  starting transfers between devices  80.6 us (24%)
  local copies, waits for them, and re-layouts  30.4 us (9%)
  between operations  14.5 us (4%)
  other arithmetic  13.3 us (4%)
  matrix products  11.8 us (4%)
    all_to_all x1, blocking collectives, shards(): spread = lax.all_to_all(partial.transpose(1, 0, 2), PAIR, 0, 0, tiled=True)  60 us
    all_to_all x1, waiting for transfers between devices, shards(): lax.all_to_all(outgoing, BEAM, split_axis=0, concat_axis=0, tiled=True)  48.4 us
    all_to_all x1, blocking collectives, shards(): arrived = lax.all_to_all(jnp.stack(cells), BEAM, 0, 0)  29.8 us
    ppermute x6, starting transfers between devices, ring_near(): return (lax.ppermute(piece, axis, ahead), lax.ppermute(piece, axis, behind))  22.8 us
    all_to_all x1, starting transfers between devices, regroup(): return lax.all_to_all(blocks, BEAM, split_axis=1, concat_axis=1, tiled=True)  22.4 us
    ppermute x3, starting transfers between devices, ring_far(): lax.ppermute(from_right[cut:], axis, behind)  13.7 us
    ppermute x6, waiting for transfers between devices, ring_near(): return (lax.ppermute(piece, axis, ahead), lax.ppermute(piece, axis, behind))  12 us
    all_to_all x1, waiting for transfers between devices, gather_rows(): lax.all_to_all(copies, axis, 0, 0, tiled=True)  10.3 us
  transfers between devices with their start and end apart: 17, of which 8 were waited for; matrix products, arithmetic and copies ran while one was open for 13% of the time, Pallas kernels for 0%

profile of v1, /device:TPU:56, one launch (start us, length us, event | category | flops | bytes accessed | tf_op | source)
XLA Modules:
  0.0 328.8 jit_solution(15406604925702332585)
XLA Ops:
  6.5 1.0 slice.65
  7.7 3.4 %collective-permute-start.3 = (bf16[512,128]{1,0:T(8,128)(2,1)S(1)}, bf16[512,128]{1,0:T(8,128)(2,1)}, u32[]{:S(2)}, u32[]{:S(2)}) collective-permute-start(bf16[512,128]{1,0:T(8,128)(2,1)S(1)} %copy.1928), channel_id=1, source_target_pairs={{0,128},{128,256},{256,384},{384,0},{1,129},{129,257},{257,385},{3... | collective-permute-start | bytes 393224 | tf_op jit(solution)/shard_map/ppermute | solution.py:43
  11.1 3.7 %collective-permute-start.4 = (bf16[512,128]{1,0:T(8,128)(2,1)S(1)}, bf16[512,128]{1,0:T(8,128)(2,1)}, u32[]{:S(2)}, u32[]{:S(2)}) collective-permute-start(bf16[512,128]{1,0:T(8,128)(2,1)S(1)} %copy.1928), channel_id=1, source_target_pairs={{0,384},{128,0},{256,128},{384,256},{1,385},{129,1},{257,129},{385... | collective-permute-start | bytes 393224 | tf_op jit(solution)/shard_map/ppermute | solution.py:43
  14.8 1.1 copy.1879
  15.9 1.9 collective-permute-start
  17.9 1.0 broadcast_in_dim.29
  18.8 7.0 %all-to-all-start = ((bf16[4,512,192]{1,2,0:T(8,128)(2,1)}), bf16[4,512,192]{1,2,0:T(8,128)(2,1)S(1)}, u32[]{:S(2)}, u32[]{:S(2)}) async-start(bf16[4,512,192]{1,2,0:T(8,128)(2,1)} %broadcast_in_dim.29), calls=%async_computation | async-start | bytes 1572864 | tf_op jit(solution)/shard_map/all_to_all | solution.py:37
  25.8 3.1 fusion
  28.9 0.5 broadcast.203
  29.5 0.7 reduce.4
  30.4 5.3 %fusion.2 = bf16[256,8192]{1,0:T(8,128)(2,1)} fusion(bf16[256,8192]{1,0:T(8,128)(2,1)} %param.10, f32[8192]{0:T(1024)S(1)} %convert_element_type.98, f32[256]{0:T(256)S(1)} %add_rsqrt_fusion), kind=kLoop, calls=%fused_computation.6 | loop fusion | flops 8388608 | bytes 8422400 | tf_op jit(solution)/shard_map/convert_element_type | solution.py:104
  35.8 10.3 %all-to-all-done = bf16[4,512,192]{1,2,0:T(8,128)(2,1)S(1)} async-done(((bf16[4,512,192]{1,2,0:T(8,128)(2,1)}), bf16[4,512,192]{1,2,0:T(8,128)(2,1)S(1)}, u32[]{:S(2)}, u32[]{:S(2)}) %all-to-all-start) | async-done | bytes 786464 | tf_op jit(solution)/shard_map/all_to_all | solution.py:37
  46.2 1.9 collective-permute-start.1
  48.1 5.1 %collective-permute-start.2 = (bf16[2048,192]{0,1:T(8,128)(2,1)S(1)}, bf16[2048,192]{0,1:T(8,128)(2,1)}, u32[]{:S(2)}, u32[]{:S(2)}) collective-permute-start(bf16[2048,192]{0,1:T(8,128)(2,1)S(1)} %bitcast.323), channel_id=1, source_target_pairs={{0,384},{128,0},{256,128},{384,256},{1,385},{129,1},{257,129},{385... | collective-permute-start | bytes 2359304 | tf_op jit(solution)/shard_map/ppermute | solution.py:43
  53.3 4.5 %constant_dynamic-slice_fusion.16 = (bf16[256,512]{1,0:T(8,128)(2,1)}, bf16[256,512]{1,0:T(8,128)(2,1)}, bf16[256,512]{1,0:T(8,128)(2,1)}, bf16[256,512]{1,0:T(8...) fusion(bf16[256,8192]{1,0:T(8,128)(2,1)} %fusion.2, ...), kind=kLoop, calls=%fused_computation.210 | loop fusion | bytes 8388672 | tf_op jit(solution)/shard_map/dynamic_slice | solution.py:135
  57.8 1.7 dynamic-slice_bitcast_fusion.2
  59.6 0.7 constant_dynamic-update-slice_fusion.4
  60.5 0.6 reshape.259
  61.1 0.8 maximum_select_fusion
  62.0 0.6 copy.1882
  62.6 0.6 reshape.346
  63.2 1.1 slice.67
  64.3 3.0 collective-permute-start.5
  67.3 1.0 slice.68
  68.4 4.0 %collective-permute-start.6 = (bf16[1024,192]{0,1:T(8,128)(2,1)S(1)}, bf16[1024,192]{0,1:T(8,128)(2,1)S(1)}, u32[]{:S(2)}, u32[]{:S(2)}) collective-permute-start(bf16[1024,192]{0,1:T(8,128)(2,1)S(1)} %slice.68), channel_id=1, source_target_pairs={{0,384},{128,0},{256,128},{384,256},{1,385},{129,1},{257,129},{385... | collective-permute-start | bytes 1179656 | tf_op jit(solution)/shard_map/ppermute | solution.py:52
  72.4 2.4 fusion.42
  74.8 2.1 fusion.46
  76.9 0.8 slice.69
  77.8 1.9 collective-permute-start.7
  79.7 0.9 constant_dynamic-update-slice_fusion.3
  80.6 0.8 slice.70
  81.5 5.1 %collective-permute-start.8 = (bf16[256,128]{1,0:T(8,128)(2,1)S(1)}, bf16[256,128]{1,0:T(8,128)(2,1)S(1)}, u32[]{:S(2)}, u32[]{:S(2)}) collective-permute-start(bf16[256,128]{1,0:T(8,128)(2,1)S(1)} %slice.70), channel_id=1, source_target_pairs={{0,384},{128,0},{256,128},{384,256},{1,385},{129,1},{257,129},{385... | collective-permute-start | bytes 196616 | tf_op jit(solution)/shard_map/ppermute | solution.py:52
  86.6 1.9 collective-permute-done.8
  88.5 0.9 constant_dynamic-update-slice_fusion
  89.4 4.2 %collective-permute-start.9 = (bf16[2048,128]{1,0:T(8,128)(2,1)S(1)}, bf16[2048,128]{1,0:T(8,128)(2,1)S(1)}, u32[]{:S(2)}, u32[]{:S(2)}) collective-permute-start(bf16[2048,128]{1,0:T(8,128)(2,1)S(1)} %constant_dynamic-update-slice_fusion), channel_id=1, source_target_pairs={{0,96},{32,0},{64,32},{96,64},{1,97},{33,1},{65,33},{97,65},{2,98}... | collective-permute-start | bytes 1572872 | tf_op jit(solution)/shard_map/ppermute | solution.py:43
  93.7 4.5 %collective-permute-start.10 = (bf16[2048,128]{1,0:T(8,128)(2,1)S(1)}, bf16[2048,128]{1,0:T(8,128)(2,1)S(1)}, u32[]{:S(2)}, u32[]{:S(2)}) collective-permute-start(bf16[2048,128]{1,0:T(8,128)(2,1)S(1)} %constant_dynamic-update-slice_fusion), channel_id=1, source_target_pairs={{0,32},{32,64},{64,96},{96,0},{1,33},{33,65},{65,97},{97,1},{2,34}... | collective-permute-start | bytes 1572872 | tf_op jit(solution)/shard_map/ppermute | solution.py:43
  98.2 0.9 fusion.44
  99.1 2.1 fusion.8
  101.2 12.0 %collective-permute-done.10 = bf16[2048,128]{1,0:T(8,128)(2,1)S(1)} collective-permute-done((bf16[2048,128]{1,0:T(8,128)(2,1)S(1)}, bf16[2048,128]{1,0:T(8,128)(2,1)S(1)}, u32[]{:S(2)}, u32[]{:S(2)}) %collective-permute-start.10) | collective-permute-done | bytes 524320 | tf_op jit(solution)/shard_map/ppermute | solution.py:43
  113.2 3.6 %collective-permute-start.11 = (bf16[1024,128]{1,0:T(8,128)(2,1)S(1)}, bf16[1024,128]{1,0:T(8,128)(2,1)S(1)}, u32[]{:S(2)}, u32[]{:S(2)}) collective-permute-start(bf16[1024,128]{1,0:T(8,128)(2,1)S(1)} %slice.101), channel_id=1, source_target_pairs={{0,32},{32,64},{64,96},{96,0},{1,33},{33,65},{65,97},{97,1},{2,34}... | collective-permute-start | bytes 786440 | tf_op jit(solution)/shard_map/ppermute | solution.py:52
  116.8 4.5 %collective-permute-start.12 = (bf16[1024,128]{1,0:T(8,128)(2,1)S(1)}, bf16[1024,128]{1,0:T(8,128)(2,1)S(1)}, u32[]{:S(2)}, u32[]{:S(2)}) collective-permute-start(bf16[1024,128]{1,0:T(8,128)(2,1)S(1)} %slice.102), channel_id=1, source_target_pairs={{0,96},{32,0},{64,32},{96,64},{1,97},{33,1},{65,33},{97,65},{2,98}... | collective-permute-start | bytes 786440 | tf_op jit(solution)/shard_map/ppermute | solution.py:52
  121.9 0.5 copy-done.12
  122.6 0.4 fusion.34
  123.1 2.7 collective-permute-done.11
  125.8 1.4 collective-permute-done.12
  127.7 0.5 copy-done.4
  128.8 0.8 pad_maximum_fusion
  129.7 22.4 %all-to-all-start.1 = ((bf16[8,32,320]{2,0,1:T(8,128)(2,1)}), bf16[8,32,320]{2,0,1:T(8,128)(2,1)S(1)}, u32[]{:S(2)}, u32[]{:S(2)}) async-start(bf16[8,32,320]{2,0,1:T(8,128)(2,1)} %pad_maximum_fusion), calls=%async_computation.1 | async-start | bytes 393216 | tf_op jit(solution)/shard_map/all_to_all | solution.py:32
  152.1 2.1 gather_fusion
  154.2 7.9 %all-to-all-done.1 = bf16[8,32,320]{2,0,1:T(8,128)(2,1)S(1)} async-done(((bf16[8,32,320]{2,0,1:T(8,128)(2,1)}), bf16[8,32,320]{2,0,1:T(8,128)(2,1)S(1)}, u32[]{:S(2)}, u32[]{:S(2)}) %all-to-all-start.1) | async-done | bytes 163872 | tf_op jit(solution)/shard_map/all_to_all | solution.py:32
  162.1 4.3 %all-to-all-start.2 = ((bf16[32,2,2,8,1024]{4,3,2,1,0:T(8,128)(2,1)}), bf16[32,2,2,8,1024]{4,3,2,1,0:T(8,128)(2,1)S(1)}, u32[]{:S(2)}, u32[]{:S(2)}) async-start(bf16[32,2,2,8,1024]{4,3,2,1,0:T(8,128)(2,1)} %bitcast.30), calls=%async_computation.2 | async-start | bytes 4194304 | tf_op jit(solution)/shard_map/all_to_all | solution.py:161
  168.0 48.4 %all-to-all-done.2 = bf16[32,2,2,8,1024]{4,3,2,1,0:T(8,128)(2,1)S(1)} async-done(((bf16[32,2,2,8,1024]{4,3,2,1,0:T(8,128)(2,1)}), bf16[32,2,2,8,1024]{4,3,2,1,0:T(8,128)(2,1)S(1)}, u32[]{:S(2)}, u32[]{:S(2)}) %all-to-all-start.2) | async-done | bytes 2097184 | tf_op jit(solution)/shard_map/all_to_all | solution.py:161
  216.4 1.6 gather_fusion.1
  218.0 1.6 copy.1930
  219.7 0.5 fusion.91
  221.4 29.8 %all_to_all.25 = bf16[32,8,1,512]{3,1,2,0:T(8,128)(2,1)S(1)} all-to-all(bf16[32,8,1,512]{3,1,2,0:T(8,128)(2,1)S(1)} %constant_dynamic-update-slice_fusion.5), channel_id=1, replica_groups=mesh['x'=4,'yh'=4,'yl'=2,'z'=8,'c'=2] {'yl','z','c'}, dimensions={0} | all-to-all | bytes 524288 | tf_op jit(solution)/shard_map/all_to_all | solution.py:185
  251.3 3.7 %all-gather.3.cloned.1.call-done = bf16[512,4096]{0,1:T(8,128)(2,1)} async-done(((bf16[512,256]{0,1:T(8,128)(2,1)}), bf16[512,4096]{0,1:T(8,128)(2,1)}) %all-gather.3.cloned.1.call-update) | async-done | bytes 4194320 | tf_op jit(solution)/shard_map/all_gather | solution.py:116
  255.1 2.5 fusion.89
  257.6 0.7 fusion.63
  258.3 0.7 fusion.3
  259.1 1.2 copy.1909
  260.3 0.7 copy.1910
  261.0 60.0 %all_to_all.26 = bf16[16,256,256]{2,1,0:T(8,128)(2,1)S(1)} all-to-all(bf16[16,256,256]{2,1,0:T(8,128)(2,1)S(1)} %copy.1910), channel_id=1, replica_groups=mesh['x'=4,'yh'=4,'yl'=2,'z'=8,'c'=2] {'yl','z'}, dimensions={0} | all-to-all | bytes 4194304 | tf_op jit(solution)/shard_map/all_to_all | solution.py:202
  321.0 1.0 reduce_sum.55
  (145 shorter events, 5.5 us)
Async XLA Ops:
  6.5 145.6 %copy-start = (bf16[32,2,8,1024]{3,2,1,0:T(8,128)(2,1)S(1)}, bf16[32,2,8,1024]{3,2,1,0:T(8,128)(2,1)}, u32[]{:S(2)}) copy-start(bf16[32,2,8,1024]{3,2,1,0:T(8,128)(2,1)} %param.14) | copy-start | bytes 3145732
  6.5 11.3 %slice-start = ((bf16[512,320]{0,1:T(8,128)(2,1)}), bf16[512,192]{0,1:T(8,128)(2,1)S(1)}, s32[]{:S(2)}) async-start(bf16[512,320]{0,1:T(8,128)(2,1)} %param.12), calls=%async_computation.6 | async-start | bytes 393216 | tf_op jit(solution)/shard_map/slice | solution.py:112
  7.7 55.5 %collective-permute-start.3 = (bf16[512,128]{1,0:T(8,128)(2,1)S(1)}, bf16[512,128]{1,0:T(8,128)(2,1)}, u32[]{:S(2)}, u32[]{:S(2)}) collective-permute-start(bf16[512,128]{1,0:T(8,128)(2,1)S(1)} %copy.1928), channel_id=1, source_target_pairs={{0,128},{128,256},{256,384},{384,0},{1,129},{129,257},{257,385},{3... | collective-permute-start | bytes 393224 | tf_op jit(solution)/shard_map/ppermute | solution.py:43
  11.1 52.1 %collective-permute-start.4 = (bf16[512,128]{1,0:T(8,128)(2,1)S(1)}, bf16[512,128]{1,0:T(8,128)(2,1)}, u32[]{:S(2)}, u32[]{:S(2)}) collective-permute-start(bf16[512,128]{1,0:T(8,128)(2,1)S(1)} %copy.1928), channel_id=1, source_target_pairs={{0,384},{128,0},{256,128},{384,256},{1,385},{129,1},{257,129},{385... | collective-permute-start | bytes 393224 | tf_op jit(solution)/shard_map/ppermute | solution.py:43
  14.8 11.0 %copy-start.21 = (bf16[8192]{0:T(1024)(128)(2,1)S(1)}, bf16[8192]{0:T(1024)(128)(2,1)}, u32[]{:S(2)}) copy-start(bf16[8192]{0:T(1024)(128)(2,1)} %param.11) | copy-start | bytes 49156
  15.9 45.2 %collective-permute-start = (bf16[256,256]{0,1:T(8,128)(2,1)S(1)}, bf16[256,256]{0,1:T(8,128)(2,1)S(1)}, u32[]{:S(2)}, u32[]{:S(2)}) collective-permute-start(bf16[256,256]{0,1:T(8,128)(2,1)S(1)} %get-tuple-element.55), channel_id=1, source_target_pairs={{0,1},{1,0},{2,3},{3,2},{4,5},{5,4},{6,7},{7,6},{8,9},{9,8},{10,11... | collective-permute-start | bytes 393224 | tf_op jit(solution)/shard_map/ppermute | solution.py:98
  18.8 27.3 %all-to-all-start = ((bf16[4,512,192]{1,2,0:T(8,128)(2,1)}), bf16[4,512,192]{1,2,0:T(8,128)(2,1)S(1)}, u32[]{:S(2)}, u32[]{:S(2)}) async-start(bf16[4,512,192]{1,2,0:T(8,128)(2,1)} %broadcast_in_dim.29), calls=%async_computation | async-start | bytes 1572864 | tf_op jit(solution)/shard_map/all_to_all | solution.py:37
  25.8 3.7 %copy-start.23 = (s32[1024,1]{0,1:T(1,128)S(1)}, s32[1024,1]{0,1:T(1,128)}, u32[]{:S(2)}) copy-start(s32[1024,1]{0,1:T(1,128)} %param.16) | copy-start | bytes 12292
  46.2 17.0 %collective-permute-start.1 = (bf16[2048,192]{0,1:T(8,128)(2,1)S(1)}, bf16[2048,192]{0,1:T(8,128)(2,1)}, u32[]{:S(2)}, u32[]{:S(2)}) collective-permute-start(bf16[2048,192]{0,1:T(8,128)(2,1)S(1)} %bitcast.322), channel_id=1, source_target_pairs={{0,128},{128,256},{256,384},{384,0},{1,129},{129,257},{257,385},{3... | collective-permute-start | bytes 2359304 | tf_op jit(solution)/shard_map/ppermute | solution.py:43
  48.1 15.1 %collective-permute-start.2 = (bf16[2048,192]{0,1:T(8,128)(2,1)S(1)}, bf16[2048,192]{0,1:T(8,128)(2,1)}, u32[]{:S(2)}, u32[]{:S(2)}) collective-permute-start(bf16[2048,192]{0,1:T(8,128)(2,1)S(1)} %bitcast.323), channel_id=1, source_target_pairs={{0,384},{128,0},{256,128},{384,256},{1,385},{129,1},{257,129},{385... | collective-permute-start | bytes 2359304 | tf_op jit(solution)/shard_map/ppermute | solution.py:43
  53.2 4.6 %copy-start.1 = (bf16[256,8192]{1,0:T(8,128)(2,1)S(1)}, bf16[256,8192]{1,0:T(8,128)(2,1)}, u32[]{:S(2)}) copy-start(bf16[256,8192]{1,0:T(8,128)(2,1)} %fusion.2) | copy-start | bytes 12582916
  57.8 2.4 copy-start.22
  63.2 11.7 %copy-start.3 = (bf16[32,8,2048]{2,1,0:T(8,128)(2,1)S(1)}, bf16[32,8,2048]{2,1,0:T(8,128)(2,1)}, u32[]{:S(2)}) copy-start(bf16[32,8,2048]{2,1,0:T(8,128)(2,1)} %get-tuple-element.31) | copy-start | bytes 3145732
  64.3 33.8 %collective-permute-start.5 = (bf16[1024,192]{0,1:T(8,128)(2,1)S(1)}, bf16[1024,192]{0,1:T(8,128)(2,1)S(1)}, u32[]{:S(2)}, u32[]{:S(2)}) collective-permute-start(bf16[1024,192]{0,1:T(8,128)(2,1)S(1)} %slice.67), channel_id=1, source_target_pairs={{0,128},{128,256},{256,384},{384,0},{1,129},{129,257},{257,385},{3... | collective-permute-start | bytes 1179656 | tf_op jit(solution)/shard_map/ppermute | solution.py:52
  68.4 29.8 %collective-permute-start.6 = (bf16[1024,192]{0,1:T(8,128)(2,1)S(1)}, bf16[1024,192]{0,1:T(8,128)(2,1)S(1)}, u32[]{:S(2)}, u32[]{:S(2)}) collective-permute-start(bf16[1024,192]{0,1:T(8,128)(2,1)S(1)} %slice.68), channel_id=1, source_target_pairs={{0,384},{128,0},{256,128},{384,256},{1,385},{129,1},{257,129},{385... | collective-permute-start | bytes 1179656 | tf_op jit(solution)/shard_map/ppermute | solution.py:52
  72.4 7.3 %copy-start.20 = (bf16[2048,128]{1,0:T(8,128)(2,1)S(1)}, bf16[2048,128]{1,0:T(8,128)(2,1)}, u32[]{:S(2)}) copy-start(bf16[2048,128]{1,0:T(8,128)(2,1)} %constant_dynamic-update-slice_fusion.4) | copy-start | bytes 1572868
  74.8 23.4 %copy-start.2 = (bf16[32,8,2048]{2,1,0:T(8,128)(2,1)S(1)}, bf16[32,8,2048]{2,1,0:T(8,128)(2,1)}, u32[]{:S(2)}) copy-start(bf16[32,8,2048]{2,1,0:T(8,128)(2,1)} %get-tuple-element.33) | copy-start | bytes 3145732
  77.8 8.8 %collective-permute-start.7 = (bf16[256,128]{1,0:T(8,128)(2,1)S(1)}, bf16[256,128]{1,0:T(8,128)(2,1)S(1)}, u32[]{:S(2)}, u32[]{:S(2)}) collective-permute-start(bf16[256,128]{1,0:T(8,128)(2,1)S(1)} %slice.69), channel_id=1, source_target_pairs={{0,128},{128,256},{256,384},{384,0},{1,129},{129,257},{257,385},{3... | collective-permute-start | bytes 196616 | tf_op jit(solution)/shard_map/ppermute | solution.py:52
  81.5 7.0 %collective-permute-start.8 = (bf16[256,128]{1,0:T(8,128)(2,1)S(1)}, bf16[256,128]{1,0:T(8,128)(2,1)S(1)}, u32[]{:S(2)}, u32[]{:S(2)}) collective-permute-start(bf16[256,128]{1,0:T(8,128)(2,1)S(1)} %slice.70), channel_id=1, source_target_pairs={{0,384},{128,0},{256,128},{384,256},{1,385},{129,1},{257,129},{385... | collective-permute-start | bytes 196616 | tf_op jit(solution)/shard_map/ppermute | solution.py:52
  89.4 27.3 %collective-permute-start.9 = (bf16[2048,128]{1,0:T(8,128)(2,1)S(1)}, bf16[2048,128]{1,0:T(8,128)(2,1)S(1)}, u32[]{:S(2)}, u32[]{:S(2)}) collective-permute-start(bf16[2048,128]{1,0:T(8,128)(2,1)S(1)} %constant_dynamic-update-slice_fusion), channel_id=1, source_target_pairs={{0,96},{32,0},{64,32},{96,64},{1,97},{33,1},{65,33},{97,65},{2,98}... | collective-permute-start | bytes 1572872 | tf_op jit(solution)/shard_map/ppermute | solution.py:43
  93.7 19.5 %collective-permute-start.10 = (bf16[2048,128]{1,0:T(8,128)(2,1)S(1)}, bf16[2048,128]{1,0:T(8,128)(2,1)S(1)}, u32[]{:S(2)}, u32[]{:S(2)}) collective-permute-start(bf16[2048,128]{1,0:T(8,128)(2,1)S(1)} %constant_dynamic-update-slice_fusion), channel_id=1, source_target_pairs={{0,32},{32,64},{64,96},{96,0},{1,33},{33,65},{65,97},{97,1},{2,34}... | collective-permute-start | bytes 1572872 | tf_op jit(solution)/shard_map/ppermute | solution.py:43
  99.1 22.3 %copy-start.16 = (bf16[256,512]{1,0:T(8,128)(2,1)S(1)}, bf16[256,512]{1,0:T(8,128)(2,1)}, u32[]{:S(2)}) copy-start(bf16[256,512]{1,0:T(8,128)(2,1)} %get-tuple-element.43) | copy-start | bytes 786436
  99.1 22.3 %copy-start.17 = (bf16[256,512]{1,0:T(8,128)(2,1)S(1)}, bf16[256,512]{1,0:T(8,128)(2,1)}, u32[]{:S(2)}) copy-start(bf16[256,512]{1,0:T(8,128)(2,1)} %get-tuple-element.44) | copy-start | bytes 786436
  99.1 22.3 %copy-start.18 = (bf16[256,512]{1,0:T(8,128)(2,1)S(1)}, bf16[256,512]{1,0:T(8,128)(2,1)}, u32[]{:S(2)}) copy-start(bf16[256,512]{1,0:T(8,128)(2,1)} %get-tuple-element.45) | copy-start | bytes 786436
  99.1 22.3 %copy-start.19 = (bf16[256,512]{1,0:T(8,128)(2,1)S(1)}, bf16[256,512]{1,0:T(8,128)(2,1)}, u32[]{:S(2)}) copy-start(bf16[256,512]{1,0:T(8,128)(2,1)} %get-tuple-element.46) | copy-start | bytes 786436
  113.2 12.6 %collective-permute-start.11 = (bf16[1024,128]{1,0:T(8,128)(2,1)S(1)}, bf16[1024,128]{1,0:T(8,128)(2,1)S(1)}, u32[]{:S(2)}, u32[]{:S(2)}) collective-permute-start(bf16[1024,128]{1,0:T(8,128)(2,1)S(1)} %slice.101), channel_id=1, source_target_pairs={{0,32},{32,64},{64,96},{96,0},{1,33},{33,65},{65,97},{97,1},{2,34}... | collective-permute-start | bytes 786440 | tf_op jit(solution)/shard_map/ppermute | solution.py:52
  116.8 10.4 %collective-permute-start.12 = (bf16[1024,128]{1,0:T(8,128)(2,1)S(1)}, bf16[1024,128]{1,0:T(8,128)(2,1)S(1)}, u32[]{:S(2)}, u32[]{:S(2)}) collective-permute-start(bf16[1024,128]{1,0:T(8,128)(2,1)S(1)} %slice.102), channel_id=1, source_target_pairs={{0,96},{32,0},{64,32},{96,64},{1,97},{33,1},{65,33},{97,65},{2,98}... | collective-permute-start | bytes 786440 | tf_op jit(solution)/shard_map/ppermute | solution.py:52
  121.4 1.0 copy-start.12
  121.4 1.0 copy-start.13
  121.4 1.1 copy-start.14
  121.4 1.2 copy-start.15
  122.6 4.6 %copy-start.8 = (bf16[256,512]{1,0:T(8,128)(2,1)S(1)}, bf16[256,512]{1,0:T(8,128)(2,1)}, u32[]{:S(2)}) copy-start(bf16[256,512]{1,0:T(8,128)(2,1)} %get-tuple-element.39) | copy-start | bytes 786436
  122.6 4.6 %copy-start.9 = (bf16[256,512]{1,0:T(8,128)(2,1)S(1)}, bf16[256,512]{1,0:T(8,128)(2,1)}, u32[]{:S(2)}) copy-start(bf16[256,512]{1,0:T(8,128)(2,1)} %get-tuple-element.40) | copy-start | bytes 786436
  122.6 4.6 %copy-start.10 = (bf16[256,512]{1,0:T(8,128)(2,1)S(1)}, bf16[256,512]{1,0:T(8,128)(2,1)}, u32[]{:S(2)}) copy-start(bf16[256,512]{1,0:T(8,128)(2,1)} %get-tuple-element.41) | copy-start | bytes 786436
  122.6 4.6 %copy-start.11 = (bf16[256,512]{1,0:T(8,128)(2,1)S(1)}, bf16[256,512]{1,0:T(8,128)(2,1)}, u32[]{:S(2)}) copy-start(bf16[256,512]{1,0:T(8,128)(2,1)} %get-tuple-element.42) | copy-start | bytes 786436
  127.2 1.0 copy-start.4
  127.2 1.0 copy-start.5
  127.2 1.1 copy-start.6
  127.2 1.2 copy-start.7
  128.4 23.7 %copy-start.24 = (s32[64,1]{0,1:T(1,128)S(1)}, s32[64,1]{0,1:T(1,128)}, u32[]{:S(2)}) copy-start(s32[64,1]{0,1:T(1,128)} %reshape.259) | copy-start | bytes 772
  129.7 32.4 %all-to-all-start.1 = ((bf16[8,32,320]{2,0,1:T(8,128)(2,1)}), bf16[8,32,320]{2,0,1:T(8,128)(2,1)S(1)}, u32[]{:S(2)}, u32[]{:S(2)}) async-start(bf16[8,32,320]{2,0,1:T(8,128)(2,1)} %pad_maximum_fusion), calls=%async_computation.1 | async-start | bytes 393216 | tf_op jit(solution)/shard_map/all_to_all | solution.py:32
  162.1 4.5 %copy-start.25 = (s32[256]{0:T(256)S(1)}, s32[256]{0:T(256)}, u32[]{:S(2)}) copy-start(s32[256]{0:T(256)} %param.15) | copy-start | bytes 3076
  162.1 54.3 %all-to-all-start.2 = ((bf16[32,2,2,8,1024]{4,3,2,1,0:T(8,128)(2,1)}), bf16[32,2,2,8,1024]{4,3,2,1,0:T(8,128)(2,1)S(1)}, u32[]{:S(2)}, u32[]{:S(2)}) async-start(bf16[32,2,2,8,1024]{4,3,2,1,0:T(8,128)(2,1)} %bitcast.30), calls=%async_computation.2 | async-start | bytes 4194304 | tf_op jit(solution)/shard_map/all_to_all | solution.py:161
  166.3 88.7 %all-gather.3.cloned.1.call-start = ((), (), s32[]{:S(2)}) async-start(), calls=%async_computation.5 | async-start | bytes 4456448 | tf_op jit(solution)/shard_map/all_gather | solution.py:116
Sparse Core Ops, SparseCore 0:
  170.2 84.8 all-gather.2
